TPU v7x, 512 devices: a whole 4x4x16 slice. The times are simulated.
512 devices in a mesh: dp: 4 (over x), ctx: 16 (over z), mp: 8 (over y, core).
Axes of the slice: x: 4, y: 4, z: 16, core: 2. Of those that a mesh axis runs over, the one named last changes fastest.
Arguments:
- tokens: bfloat16 [4, 2048, 4096], P('dp', 'ctx'), may hold values from -52 to 52
- x_weight: bfloat16 [4096, 8192], P(('dp', 'ctx'), 'mp'), may hold values from -0.09375 to 0.09375
- bc_weight: bfloat16 [4096, 1024], P(('dp', 'ctx'), 'mp'), may hold values from -0.09375 to 0.09375
- dt_weight: bfloat16 [4096, 128], P(('dp', 'ctx'), 'mp'), may hold values from -0.0234375 to 0.0234375
- conv_x: float32 [5, 8192], P(None, 'mp'), may hold values from -0.5 to 0.5
- conv_bc: float32 [5, 1024], P(None, 'mp'), may hold values from -0.5 to 0.5
- dt_bias: float32 [128], P('mp'), may hold values from -4.5 to -2.5
- a_log: float32 [128], P('mp')
- d_skip: float32 [128], P('mp'), may hold values from 0.5 to 1.5
- norm_gain: float32 [8192], P('mp'), may hold values from 0.5 to 1.5
Outputs:
- mixer_out: bfloat16 [4, 2048, 8192], P('dp', 'ctx', 'mp')
- kurtosis: float32 [4096], P('mp')
All inputs are finite; a program needn't handle non-finite values.
Results may differ from a plain program's by a relative error of at most 0.015.
Values may be sent and summed in bfloat16 or wider, within the bound.
No kernel may reach another device: no remote copies, remote signals or barrier semaphores. Data moves between devices by JAX's collectives and lax.ppermute only.
A program may use at most 64 MiB of HBM per device.

v0:
```python
import jax
import jax.numpy as jnp
from jax import lax
from jax.sharding import PartitionSpec as P

ROOT = 64
HEADS = 128
G = 4
NS = 128
HIGH = lax.Precision.HIGHEST


def passed_along(value, axis, steps):
    count = lax.axis_size(axis)
    first, last = (max(0, -steps), min(count, count - steps))
    return lax.ppermute(value, axis, [(source, source + steps) for source in range(first, last)])


def entering(array, axis, combine, identity):
    length, place = (lax.axis_size(axis), lax.axis_index(axis))
    everything = jax.tree.map(
        lambda part, kind: lax.all_gather(part.astype(kind), axis),
        array,
        (jnp.bfloat16, jnp.bfloat16),
    )
    start = jax.tree.map(
        lambda part, zero: jnp.broadcast_to(jnp.asarray(zero, part.dtype), part.shape),
        array,
        identity,
    )

    def step(k, before):
        reached = k < place
        new = combine(
            before, jax.tree.map(lambda part, own: part[k].astype(own.dtype), everything, array)
        )
        return jax.tree.map(lambda a, b: jnp.where(reached, a, b), new, before)

    return lax.fori_loop(0, length, step, start)


def hadamard_signs(sign_order):
    row_index = lax.broadcasted_iota(jnp.int32, (sign_order, sign_order), 0)
    col_index = lax.broadcasted_iota(jnp.int32, (sign_order, sign_order), 1)
    common = jnp.bitwise_and(row_index, col_index)
    parity = jnp.zeros((sign_order, sign_order), jnp.int32)
    for bit_index in range(sign_order.bit_length() - 1):
        parity = parity + jnp.bitwise_and(jnp.right_shift(common, bit_index), 1)
    return 1.0 - 2.0 * jnp.bitwise_and(parity, 1).astype(jnp.float32)


def kurtosis_from(powers, row_count):
    average = powers[0] / row_count
    second = powers[1] / row_count - average * average
    fourth = (
        powers[3] / row_count
        - 4.0 * average * powers[2] / row_count
        + 6.0 * average * average * powers[1] / row_count
        - 3.0 * average * average * average * average
    )
    return fourth / (second * second + 1e-06)


def chain_states(earlier, later):
    return (earlier[0] * later[0], later[0][:, :, None, None] * earlier[1] + later[1])


def shards(
    tokens, x_weight, bc_weight, dt_weight, conv_x, conv_bc, dt_bias, a_log, d_skip, norm_gain
):
    tok_rows = tokens.shape[1]
    model_width = tokens.shape[2]
    signs = hadamard_signs(ROOT)
    blocks = tokens.reshape(tok_rows, ROOT, ROOT)
    first_pass = jnp.einsum(
        "tab,ac->tcb", blocks, signs.astype(jnp.bfloat16), preferred_element_type=jnp.float32
    )
    second = jnp.einsum("tcb,bd->tcd", first_pass, signs, precision=HIGH)
    rotated = (second.reshape(tok_rows, model_width) / ROOT).astype(jnp.bfloat16)
    channel_share = model_width // lax.axis_size("mp")
    own_cols = lax.dynamic_slice_in_dim(
        rotated, lax.axis_index("mp") * channel_share, channel_share, 1
    ).astype(jnp.float32)
    square = own_cols * own_cols
    powers = jnp.stack(
        [
            jnp.sum(own_cols, 0),
            jnp.sum(square, 0),
            jnp.sum(square * own_cols, 0),
            jnp.sum(square * square, 0),
        ]
    )
    row_count = float(tok_rows * lax.axis_size("dp") * lax.axis_size("ctx"))
    totals = lax.psum(powers, ("dp", "ctx"))
    kurtosis = kurtosis_from(totals, row_count)
    panels = (
        lax.all_gather(x_weight, ("dp", "ctx"), axis=0, tiled=True),
        lax.all_gather(bc_weight, ("dp", "ctx"), axis=0, tiled=True),
        lax.all_gather(dt_weight, ("dp", "ctx"), axis=0, tiled=True),
    )
    projected = tuple(
        (jnp.dot(rotated, panel, preferred_element_type=jnp.float32) for panel in panels)
    )
    x_cols = x_weight.shape[1]
    joined = jnp.concatenate(
        [projected[0].astype(jnp.bfloat16), projected[1].astype(jnp.bfloat16)], 1
    )
    dt_proj = lax.optimization_barrier(projected[2].astype(jnp.bfloat16))
    conv_taps = jnp.concatenate([conv_x, conv_bc], 1)
    kernel = conv_taps.shape[0] - 1
    rim_rows = passed_along(joined[tok_rows - (kernel - 1) :], "ctx", 1)
    padded = jnp.concatenate([rim_rows, joined], 0)
    conv_sum = conv_taps[kernel]
    for tap_index in range(kernel):
        conv_sum = conv_sum + conv_taps[tap_index] * padded[tap_index : tap_index + tok_rows]
    convolved = jax.nn.silu(conv_sum).astype(jnp.bfloat16)
    x_conv = convolved[:, :x_cols]
    group_all = lax.all_gather(convolved[:, x_cols:], "mp", axis=1, tiled=True)
    heads_dev = dt_weight.shape[1]
    head_size = x_cols // heads_dev
    per_group = HEADS // G
    groups_here = max(1, heads_dev // per_group)
    heads_local = heads_dev // groups_here
    first_group = lax.axis_index("mp") * heads_dev // per_group
    write_all = group_all[:, : G * NS].reshape(tok_rows, G, NS)
    read_all = group_all[:, G * NS :].reshape(tok_rows, G, NS)
    write_here = lax.dynamic_slice_in_dim(write_all, first_group, groups_here, 1)
    read_here = lax.dynamic_slice_in_dim(read_all, first_group, groups_here, 1)
    step_size = jax.nn.softplus(dt_proj.astype(jnp.float32) + dt_bias)
    decay_rate = step_size * jnp.exp(a_log)
    cumulative = jnp.cumsum(decay_rate, 0)
    block_end = cumulative[-1]
    causal = lax.broadcasted_iota(jnp.int32, (tok_rows, tok_rows), 0) >= lax.broadcasted_iota(
        jnp.int32, (tok_rows, tok_rows), 1
    )
    spread = cumulative.T[:, :, None] - cumulative.T[:, None, :]
    decay_mask = jnp.where(causal, jnp.exp(-jnp.where(causal, spread, 0.0)), 0.0)
    scores = jnp.einsum("tgn,sgn->gts", read_here, write_here, preferred_element_type=jnp.float32)
    weights = (
        scores[:, None]
        * decay_mask.reshape(groups_here, heads_local, tok_rows, tok_rows)
        * step_size.T.reshape(groups_here, heads_local, 1, tok_rows)
    ).astype(jnp.bfloat16)
    x_heads = x_conv.reshape(tok_rows, groups_here, heads_local, head_size)
    within_block = jnp.einsum(
        "ghts,sghp->tghp", weights, x_heads, preferred_element_type=jnp.float32
    )
    update = (
        (jnp.exp(-(block_end - cumulative)) * step_size).reshape(
            tok_rows, groups_here, heads_local
        )[..., None]
        * x_heads
    ).astype(jnp.bfloat16)
    contrib = jnp.einsum("sghp,sgn->ghpn", update, write_here, preferred_element_type=jnp.float32)
    identity = (jnp.ones((groups_here, heads_local), jnp.float32), jnp.zeros_like(contrib))
    carried = entering(
        (jnp.exp(-block_end).reshape(groups_here, heads_local), contrib),
        "ctx",
        chain_states,
        identity,
    )
    from_before = jnp.exp(-cumulative).reshape(tok_rows, groups_here, heads_local)[
        ..., None
    ] * jnp.einsum("tgn,ghpn->tghp", read_here.astype(jnp.float32), carried[1], precision=HIGH)
    output_raw = (
        within_block
        + from_before
        + d_skip.reshape(groups_here, heads_local)[None, :, :, None] * x_heads.astype(jnp.float32)
    )
    mean_square = jnp.mean(output_raw * output_raw, -1, keepdims=True)
    normed = (
        output_raw
        * lax.rsqrt(mean_square + 1e-05)
        * norm_gain.reshape(groups_here, heads_local, head_size)
    )
    return (normed.reshape(1, tok_rows, x_cols).astype(jnp.bfloat16), kurtosis)


def solution(mesh):
    return jax.shard_map(
        shards,
        mesh=mesh,
        in_specs=(
            P("dp", "ctx", None),
            P(("dp", "ctx"), "mp"),
            P(("dp", "ctx"), "mp"),
            P(("dp", "ctx"), "mp"),
            P(None, "mp"),
            P(None, "mp"),
            P("mp"),
            P("mp"),
            P("mp"),
            P("mp"),
        ),
        out_specs=(P("dp", "ctx", "mp"), P("mp")),
        check_vma=False,
    )
```

profile of v0, /device:TPU:8, one launch (start us, length us, event | category | flops | bytes accessed | tf_op | source)
XLA Modules:
  0.0 532.6 jit_solution(13258673937758941600)
XLA Ops:
  7.2 0.7 all-gather.10.cloned.1.call-update
  8.0 0.7 all-gather.8.cloned.1.call-update
  8.7 1.6 copy.40
  10.3 88.7 %all-gather.2 = bf16[64,64,16]{1,2,0:T(8,128)(2,1)S(1)} all-gather(bf16[1,64,16]{1,2,0:T(8,128)(2,1)S(1)} %bitcast.105), channel_id=1, replica_groups=mesh['dp'=4,'ctx'=16,'mp'=8] {'dp','ctx'}, dimensions={0}, use_global_device_ids=true | all-gather | bytes 133120 | tf_op jit(solution)/shard_map/all_gather | solution.py:99
  99.1 0.3 reshape.184
  99.4 0.9 convolution_bitcast_fusion
  100.4 3.3 multiply_convert_fusion
  103.7 0.3 convolution_convert_fusion.3
  104.2 0.2 reduce_window_sum.11
  104.5 49.7 %all-gather.10.cloned.1.call-done = bf16[4096,128]{1,0:T(8,128)(2,1)} async-done(((bf16[64,128]{1,0:T(8,128)(2,1)}), bf16[4096,128]{1,0:T(8,128)(2,1)}) %all-gather.10.cloned.1.call-update) | async-done | bytes 1048592 | tf_op jit(solution)/shard_map/all_gather | solution.py:98
  154.2 1.7 convolution_convert_fusion.2
  155.9 154.7 %all-gather.8.cloned.1.call-done = bf16[4096,1024]{1,0:T(8,128)(2,1)} async-done(((bf16[64,1024]{1,0:T(8,128)(2,1)}), bf16[4096,1024]{1,0:T(8,128)(2,1)}) %all-gather.8.cloned.1.call-update) | async-done | bytes 8388624 | tf_op jit(solution)/shard_map/all_gather | solution.py:97
  310.6 4.7 convolution_convert_fusion.1
  315.3 3.7 collective-permute-start
  319.1 0.2 copy.53
  319.3 1.0 collective-permute-done
  320.4 0.4 multiply_convert_fusion.2
  320.9 11.9 %all_gather.26 = bf16[128,1024]{1,0:T(8,128)(2,1)S(1)} all-gather(bf16[128,128]{1,0:T(8,128)(2,1)S(1)} %slice.84), channel_id=1, replica_groups=mesh['dp'=4,'ctx'=16,'mp'=8] {'mp'}, dimensions={1}, use_global_device_ids=true | all-gather | bytes 294912 | tf_op jit(solution)/shard_map/all_gather | solution.py:118
  332.9 0.2 copy.54
  333.2 0.9 convolution_convert_fusion
  334.3 28.7 %all-gather.3 = bf16[16,1,16]{2,1,0:T(2,128)(2,1)S(1)} all-gather(bf16[1,1,16]{2,1,0:T(2,128)(2,1)S(1)} %get-tuple-element.160), channel_id=2, replica_groups=mesh['dp'=4,'ctx'=16,'mp'=8] {'ctx'}, dimensions={0}, use_global_device_ids=true | all-gather | bytes 544 | tf_op jit(solution)/shard_map/all_gather | solution.py:22
  363.0 0.3 convert_reduce_fusion
  363.4 141.2 %psum.7 = f32[4,512]{1,0:T(4,128)S(1)} all-reduce(f32[4,512]{1,0:T(4,128)S(1)} %pad_maximum_fusion.1), channel_id=1, replica_groups=mesh['dp'=4,'ctx'=16,'mp'=8] {'dp','ctx'}, use_global_device_ids=true, to_apply=%region_8.9 | all-reduce | flops 2048 | bytes 16384 | tf_op jit(solution)/shard_map/psum | solution.py:94
  504.6 0.6 fusion.34
  505.3 0.2 copy.56
  505.5 0.2 copy.44
  505.7 0.1 fusion.22
  505.9 18.1 %while.14 = (s32[]{:T(128)}, f32[1,16,64,128]{3,2,1,0:T(8,128)S(1)}, s32[]{:T(128)}, bf16[16,1,16]{2,1,0:T(2,128)(2,1)S(1)}, bf16[16,1,16,64,128]{4,3,2,1,0:T(8,128)(2,1)}, /*index=5*/s32[]{:T(128)}, s32[]{:T(128)}) while((s32[]{:T(128)}, f32[1,16,64,128]{3,2,1,0:T(8,128)S(1)}, s32[]{:T(128)}, bf16[16,1,16]{2,1,0:T(2,128)(2,1)S(1)}, ...), condition=%wide.region_2.0_spmd.clone, body=%wide.region_1.0_spmd.clone.sunk | while | flops 655380 | bytes 1310985 | solution.py:39
  505.9 1.1 fusion.65
  507.1 1.1 fusion.65
  508.2 1.1 fusion.65
  509.3 1.1 fusion.65
  510.5 1.1 fusion.65
  511.6 1.1 fusion.65
  512.7 1.1 fusion.65
  513.8 1.1 fusion.65
  515.0 1.1 fusion.65
  516.1 1.1 fusion.65
  517.2 1.1 fusion.65
  518.4 1.1 fusion.65
  519.5 1.1 fusion.65
  520.6 1.1 fusion.65
  521.8 1.1 fusion.65
  522.9 1.1 fusion.65
  524.0 0.4 fusion.7
  524.4 0.6 multiply_reduce_fusion
  525.0 0.2 multiply_convert_fusion.4
  525.2 0.9 copy.57
  (65 shorter events, 1.5 us)
Async XLA Ops:
  7.2 3.2 copy-start.1
  7.2 147.1 %all-gather.10.cloned.1.call-start = ((), (), s32[]{:S(2)}) async-start(), calls=%async_computation.1 | async-start | bytes 1064960 | tf_op jit(solution)/shard_map/all_gather | solution.py:98
  7.9 302.7 %all-gather.8.cloned.1.call-start = ((), (), s32[]{:S(2)}) async-start(), calls=%async_computation | async-start | bytes 8519680 | tf_op jit(solution)/shard_map/all_gather | solution.py:97
  8.7 497.2 %all-gather.12.cloned.1.call-start = ((), (), s32[]{:S(2)}) async-start(), calls=%async_computation.2 | async-start | bytes 4456448 | tf_op jit(solution)/shard_map/all_gather | solution.py:22
  100.3 3.6 copy-start.5
  100.3 3.6 copy-start.4
  100.3 4.0 copy-start
  100.3 4.1 copy-start.3
  315.3 5.1 collective-permute-start
  320.8 13.4 %copy-start.2 = (f32[1024]{0:T(1024)S(1)}, f32[1024]{0:T(1024)}, u32[]{:S(2)}) copy-start(f32[1024]{0:T(1024)} %param.21) | copy-start | bytes 12292
  505.9 18.5 %copy-start.6 = (f32[16]{0:T(128)S(1)}, f32[16]{0:T(128)}, u32[]{:S(2)}) copy-start(f32[16]{0:T(128)} %param.20) | copy-start | bytes 196
Sparse Core Ops, SparseCore 0:
  10.9 143.2 all-gather.9
  157.2 153.3 all-gather.7
  334.2 75.3 all-gather.11
where the time goes:
time: 533 us
  blocking collectives  271 us (51%)
  waiting for transfers between devices  207 us (39%)
  other arithmetic  19.7 us (4%)
  between operations  14.1 us (3%)
  matrix products  12.9 us (2%)
    all_gather x1, waiting for transfers between devices, shards(): lax.all_gather(x_weight, ('dp', 'ctx'), axis=0, tiled=True)  155 us
    psum x1, blocking collectives, shards(): totals = lax.psum(powers, ('dp', 'ctx'))  141 us
    all_gather x1, blocking collectives, shards(): lax.all_gather(dt_weight, ('dp', 'ctx'), axis=0, tiled=True)  88.7 us
    all_gather x1, waiting for transfers between devices, shards(): lax.all_gather(bc_weight, ('dp', 'ctx'), axis=0, tiled=True)  49.7 us
    all_gather x1, blocking collectives, entering(): lax.all_gather(part.astype(kind), axis)  28.7 us
    select_n x16, other arithmetic, step(): return jax.tree.map(lambda a, b: jnp.where(reached, a, b), new, before)  17.5 us
    all_gather x1, blocking collectives, shards(): group_all = lax.all_gather(convolved[:, x_cols:], 'mp', axis=1, tiled=True)  11.9 us
  transfers between devices with their start and end apart: 4, of which 3 were waited for; matrix products, arithmetic and copies ran while one was open for 2% of the time, Pallas kernels for 0%

commit v1 on v0

--- a/solution.py
+++ b/solution.py
@@ -91,7 +91,7 @@
         ]
     )
     row_count = float(tok_rows * lax.axis_size("dp") * lax.axis_size("ctx"))
-    totals = lax.psum(powers, ("dp", "ctx"))
+    totals = lax.psum(lax.psum(powers, "ctx"), "dp")
     kurtosis = kurtosis_from(totals, row_count)
     panels = (
         lax.all_gather(x_weight, ("dp", "ctx"), axis=0, tiled=True),

time: 533 us -> 437 us (0.82)
  the two profiles are of different devices: /device:TPU:8 before, /device:TPU:2 now
where the time goes in v1:
time: 437 us; the launch traced here: 436 us
  waiting for transfers between devices  214 us (49%)
  blocking collectives  167 us (38%)
  other arithmetic  19.7 us (5%)
  between operations  14.1 us (3%)
  matrix products  12.9 us (3%)
    all_gather x1, waiting for transfers between devices, shards(): lax.all_gather(x_weight, ('dp', 'ctx'), axis=0, tiled=True)  154 us
    all_gather x1, blocking collectives, shards(): lax.all_gather(dt_weight, ('dp', 'ctx'), axis=0, tiled=True)  88.2 us
    all_gather x1, waiting for transfers between devices, shards(): lax.all_gather(bc_weight, ('dp', 'ctx'), axis=0, tiled=True)  49.3 us
    psum x2, blocking collectives, shards(): totals = lax.psum(lax.psum(powers, 'ctx'), 'dp')  37.8 us
    all_gather x1, blocking collectives, entering(): lax.all_gather(part.astype(kind), axis)  28.9 us
    select_n x16, other arithmetic, step(): return jax.tree.map(lambda a, b: jnp.where(reached, a, b), new, before)  17.5 us
    all_gather x1, blocking collectives, shards(): group_all = lax.all_gather(convolved[:, x_cols:], 'mp', axis=1, tiled=True)  12.2 us
  transfers between devices with their start and end apart: 4, of which 4 were waited for; matrix products, arithmetic and copies ran while one was open for 2% of the time, Pallas kernels for 0%

profile of v1, /device:TPU:2, one launch (start us, length us, event | category | flops | bytes accessed | tf_op | source)
XLA Modules:
  0.0 436.1 jit_solution(16806582618265959157)
XLA Ops:
  7.2 0.7 all-gather.10.cloned.1.call-update
  8.0 0.7 all-gather.8.cloned.1.call-update
  8.7 1.6 copy.40
  10.3 88.2 %all-gather.2 = bf16[64,64,16]{1,2,0:T(8,128)(2,1)S(1)} all-gather(bf16[1,64,16]{1,2,0:T(8,128)(2,1)S(1)} %bitcast.105), channel_id=1, replica_groups=mesh['dp'=4,'ctx'=16,'mp'=8] {'dp','ctx'}, dimensions={0}, use_global_device_ids=true | all-gather | bytes 133120 | tf_op jit(solution)/shard_map/all_gather | solution.py:99
  98.6 0.3 reshape.184
  98.9 0.9 convolution_bitcast_fusion
  99.9 3.3 multiply_convert_fusion
  103.2 0.2 convolution_convert_fusion.3
  103.6 0.2 reduce_window_sum.11
  104.0 49.3 %all-gather.10.cloned.1.call-done = bf16[4096,128]{1,0:T(8,128)(2,1)} async-done(((bf16[64,128]{1,0:T(8,128)(2,1)}), bf16[4096,128]{1,0:T(8,128)(2,1)}) %all-gather.10.cloned.1.call-update) | async-done | bytes 1048592 | tf_op jit(solution)/shard_map/all_gather | solution.py:98
  153.3 1.7 convolution_convert_fusion.2
  155.0 154.5 %all-gather.8.cloned.1.call-done = bf16[4096,1024]{1,0:T(8,128)(2,1)} async-done(((bf16[64,1024]{1,0:T(8,128)(2,1)}), bf16[4096,1024]{1,0:T(8,128)(2,1)}) %all-gather.8.cloned.1.call-update) | async-done | bytes 8388624 | tf_op jit(solution)/shard_map/all_gather | solution.py:97
  309.5 4.7 %convolution_convert_fusion.1 = bf16[128,1024]{1,0:T(8,128)(2,1)S(1)} fusion(bf16[128,4096]{0,1:T(8,128)(2,1)S(1)} %bitcast.86, bf16[4096,1024]{1,0:T(8,128)(2,1)} %all-gather.8.cloned.1.call-done), kind=kOutput, calls=%fused_computation.13 | convolution fusion | flops 1073872896 | bytes 9699328 | tf_op jit(solution)/shard_map/dot_general | solution.py:102
  314.2 3.7 collective-permute-start
  318.0 0.2 copy.53
  318.2 1.0 collective-permute-done
  319.3 0.4 multiply_convert_fusion.2
  319.7 12.2 %all_gather.26 = bf16[128,1024]{1,0:T(8,128)(2,1)S(1)} all-gather(bf16[128,128]{1,0:T(8,128)(2,1)S(1)} %slice.84), channel_id=1, replica_groups=mesh['dp'=4,'ctx'=16,'mp'=8] {'mp'}, dimensions={1}, use_global_device_ids=true | all-gather | bytes 294912 | tf_op jit(solution)/shard_map/all_gather | solution.py:118
  332.3 0.9 convolution_convert_fusion
  333.5 28.9 %all-gather.3 = bf16[16,1,16]{2,1,0:T(2,128)(2,1)S(1)} all-gather(bf16[1,1,16]{2,1,0:T(2,128)(2,1)S(1)} %get-tuple-element.160), channel_id=2, replica_groups=mesh['dp'=4,'ctx'=16,'mp'=8] {'ctx'}, dimensions={0}, use_global_device_ids=true | all-gather | bytes 544 | tf_op jit(solution)/shard_map/all_gather | solution.py:22
  362.4 0.3 convert_reduce_fusion
  362.7 27.8 %psum.14 = f32[4,512]{1,0:T(4,128)S(1)} all-reduce(f32[4,512]{1,0:T(4,128)S(1)} %pad_maximum_fusion.1), channel_id=1, replica_groups=mesh['dp'=4,'ctx'=16,'mp'=8] {'ctx'}, use_global_device_ids=true, to_apply=%region_8.9 | all-reduce | flops 2048 | bytes 16384 | tf_op jit(solution)/shard_map/psum | solution.py:94
  390.6 10.0 %psum.15 = f32[4,512]{1,0:T(4,128)S(1)} all-reduce(f32[4,512]{1,0:T(4,128)S(1)} %psum.14), channel_id=1, replica_groups=mesh['dp'=4,'ctx'=16,'mp'=8] {'dp'}, use_global_device_ids=true, to_apply=%region_9.10 | all-reduce | flops 2048 | bytes 16384 | tf_op jit(solution)/shard_map/psum | solution.py:94
  400.6 0.6 fusion.34
  401.3 0.2 copy.56
  401.5 0.2 copy.44
  401.9 7.5 %all-gather.12.cloned.1.call-done = bf16[256,64,128]{2,1,0:T(8,128)(2,1)} async-done(((bf16[16,64,128]{2,1,0:T(8,128)(2,1)}), bf16[256,64,128]{2,1,0:T(8,128)(2,1)}) %all-gather.12.cloned.1.call-update) | async-done | bytes 4194320 | tf_op jit(solution)/shard_map/all_gather | solution.py:22
  409.5 18.1 %while.14 = (s32[]{:T(128)}, f32[1,16,64,128]{3,2,1,0:T(8,128)S(1)}, s32[]{:T(128)}, bf16[16,1,16]{2,1,0:T(2,128)(2,1)S(1)}, bf16[16,1,16,64,128]{4,3,2,1,0:T(8,128)(2,1)}, /*index=5*/s32[]{:T(128)}, s32[]{:T(128)}) while((s32[]{:T(128)}, f32[1,16,64,128]{3,2,1,0:T(8,128)S(1)}, s32[]{:T(128)}, bf16[16,1,16]{2,1,0:T(2,128)(2,1)S(1)}, ...), condition=%wide.region_2.0_spmd.clone, body=%wide.region_1.0_spmd.clone.sunk | while | flops 655380 | bytes 1310985 | solution.py:39
  409.5 1.1 fusion.65
  410.6 1.1 fusion.65
  411.7 1.1 fusion.65
  412.9 1.1 fusion.65
  414.0 1.1 fusion.65
  415.1 1.1 fusion.65
  416.3 1.1 fusion.65
  417.4 1.1 fusion.65
  418.5 1.1 fusion.65
  419.6 1.1 fusion.65
  420.8 1.1 fusion.65
  421.9 1.1 fusion.65
  423.0 1.1 fusion.65
  424.2 1.1 fusion.65
  425.3 1.1 fusion.65
  426.4 1.1 fusion.65
  427.5 0.4 fusion.7
  427.9 0.6 multiply_reduce_fusion
  428.6 0.2 multiply_convert_fusion.4
  428.8 0.9 copy.57
  (66 shorter events, 1.8 us)
Async XLA Ops:
  7.2 3.2 copy-start.1
  7.2 146.1 %all-gather.10.cloned.1.call-start = ((), (), s32[]{:S(2)}) async-start(), calls=%async_computation.1 | async-start | bytes 1064960 | tf_op jit(solution)/shard_map/all_gather | solution.py:98
  7.9 301.6 %all-gather.8.cloned.1.call-start = ((), (), s32[]{:S(2)}) async-start(), calls=%async_computation | async-start | bytes 8519680 | tf_op jit(solution)/shard_map/all_gather | solution.py:97
  8.7 400.8 %all-gather.12.cloned.1.call-start = ((), (), s32[]{:S(2)}) async-start(), calls=%async_computation.2 | async-start | bytes 4456448 | tf_op jit(solution)/shard_map/all_gather | solution.py:22
  99.8 3.6 copy-start.5
  99.8 3.6 copy-start.4
  99.8 4.0 copy-start
  99.8 4.1 copy-start.3
  314.2 5.0 %collective-permute-start = (bf16[3,1152]{1,0:T(4,128)(2,1)S(1)}, bf16[3,1152]{1,0:T(4,128)(2,1)S(1)}, u32[]{:S(2)}, u32[]{:S(2)}) collective-permute-start(bf16[3,1152]{1,0:T(4,128)(2,1)S(1)} %fusion.32), channel_id=1, source_target_pairs={{0,8},{8,16},{16,24},{24,32},{32,40},{40,48},{48,56},{56,64},{64,7... | collective-permute-start | bytes 20744 | tf_op jit(solution)/shard_map/ppermute | solution.py:16
  319.7 13.7 %copy-start.2 = (f32[1024]{0:T(1024)S(1)}, f32[1024]{0:T(1024)}, u32[]{:S(2)}) copy-start(f32[1024]{0:T(1024)} %param.21) | copy-start | bytes 12292
  409.5 18.5 %copy-start.6 = (f32[16]{0:T(128)S(1)}, f32[16]{0:T(128)}, u32[]{:S(2)}) copy-start(f32[16]{0:T(128)} %param.20) | copy-start | bytes 196
Sparse Core Ops, SparseCore 0:
  10.9 142.3 all-gather.9
  156.3 153.1 all-gather.7
  333.4 76.0 all-gather.11
